TPU v7x, 32 devices: a whole 2x2x4 slice. The times are simulated.
32 devices in a mesh: pw: 8 (over z, y), band: 4 (over x, core).
Axes of the slice: x: 2, y: 2, z: 4, core: 2. Of those that a mesh axis runs over, the one named last changes fastest.
Arguments:
- psi_block: float32 [2, 8, 256, 128], P(None, 'band', 'pw'), may hold values from -6 to 6
- psi_all: bfloat16 [2, 1024, 256, 128], P(None, 'band', 'pw'), may hold values from -0.0234375 to 0.0234375
- potential: float32 [128, 128, 128], P('pw'), may hold values from -8 to 8
- stick_col: int32 [256], replicated, may hold values from 0 to 16383, as said below
Outputs:
- intersection: float32 [2, 8, 1024], P(None, 'pw', 'band')
- hpsi: float32 [2, 8, 256, 128], P(None, 'band', 'pw')
Inputs may be any that keep to these rules, and one draw needn't show every extreme that they name: `stick_col`: distinct columns of the 128 x 128 plane; column 0 and column 16383 are always among them.
All inputs are finite; a program needn't handle non-finite values.
Results may differ from a plain program's by a relative error of at most 0.0029.
Values may be sent and summed in bfloat16 or wider, within the bound.
No kernel may reach another device: no remote copies, remote signals or barrier semaphores. Data moves between devices by JAX's collectives and lax.ppermute only.
A program may use at most 64 MiB of HBM per device.

v0:
```python
import math
import jax
import jax.numpy as jnp
from jax import lax
from jax.sharding import PartitionSpec as P


def frequency(index, size):
    return jnp.where(index < size // 2, index, index - size)


def kinetic_table(columns, grid_size):
    col_x = frequency(columns // grid_size, grid_size).astype(jnp.float32)
    col_y = frequency(columns % grid_size, grid_size).astype(jnp.float32)
    along = frequency(jnp.arange(grid_size, dtype=jnp.int32), grid_size).astype(jnp.float32)
    plane = col_x * col_x + col_y * col_y
    return 4.0 * (plane[:, None] + along[None, :] * along[None, :]) / float(grid_size * grid_size)


def dft_table(grid_size, sign):
    indices = jnp.arange(grid_size, dtype=jnp.int32)
    products = indices[:, None] * indices[None, :] % grid_size
    angles = 2.0 * math.pi / grid_size * products.astype(jnp.float32)
    cosine = jnp.cos(angles)
    sine = sign * jnp.sin(angles)
    return jnp.stack([jnp.stack([cosine, -sine]), jnp.stack([sine, cosine])])


def per_device(psi_block, psi_all, potential, stick_col):
    local_bands = psi_block.shape[1]
    sticks_dev = psi_block.shape[2]
    grid_size = psi_block.shape[3]
    highest = lax.Precision.HIGHEST
    rank = lax.axis_index("pw")
    pw_count = lax.axis_size("pw")
    band_count = lax.axis_size("band")
    my_columns = lax.dynamic_slice_in_dim(stick_col, rank * sticks_dev, sticks_dev)
    kinetic = kinetic_table(my_columns, grid_size)
    inverse = dft_table(grid_size, 1.0)
    forward = dft_table(grid_size, -1.0)
    cosine = inverse[0, 0]
    sine = inverse[1, 0]
    grid_iota = jnp.arange(grid_size, dtype=jnp.int32)
    col_x = stick_col // grid_size
    col_y = stick_col % grid_size
    phase_angles = (
        2.0
        * math.pi
        / grid_size
        * (grid_iota[:, None] * col_y[None, :] % grid_size).astype(jnp.float32)
    )
    phase_cos = jnp.cos(phase_angles)
    phase_sin = jnp.sin(phase_angles)
    place_rows = (col_x[:, None] == grid_iota[None, :]).astype(jnp.float32)
    pick_rows = (grid_iota[:, None] == col_x[None, :]).astype(jnp.float32)
    turned_pot = (jnp.transpose(potential, (0, 2, 1)) / float(grid_size**3))[None]

    def mult(left, right):
        return jnp.dot(left, right, precision=highest, preferred_element_type=jnp.float32)

    all_re = psi_all[0].reshape(psi_all.shape[1], -1)
    all_im = psi_all[1].reshape(psi_all.shape[1], -1)
    dims = (((1,), (1,)), ((), ()))
    group_count = local_bands // 2
    z_lines = jnp.einsum("dcvu,cbsu->bvds", inverse, psi_block, precision=highest)
    planes_in = lax.all_to_all(z_lines, "pw", split_axis=1, concat_axis=3, tiled=True)
    val_re = planes_in[:, :, 0, None, :]
    val_im = planes_in[:, :, 1, None, :]
    spread_re = val_re * phase_cos - val_im * phase_sin
    spread_im = val_re * phase_sin + val_im * phase_cos
    rows_re = mult(spread_re, place_rows)
    rows_im = mult(spread_im, place_rows)
    wave_re = (mult(rows_re, cosine) - mult(rows_im, sine)) * turned_pot
    wave_im = (mult(rows_re, sine) + mult(rows_im, cosine)) * turned_pot
    back_re = mult(wave_re, cosine) + mult(wave_im, sine)
    back_im = mult(wave_im, cosine) - mult(wave_re, sine)
    sel_re = mult(back_re, pick_rows)
    sel_im = mult(back_im, pick_rows)
    picked_re = jnp.sum(sel_re * phase_cos + sel_im * phase_sin, axis=2)
    picked_im = jnp.sum(sel_im * phase_cos - sel_re * phase_sin, axis=2)
    picked = jnp.stack([picked_re, picked_im], axis=2)
    sticks_back = lax.all_to_all(picked, "pw", split_axis=3, concat_axis=1, tiled=True)
    vpsi = jnp.einsum("dcvu,bucs->dbsv", forward, sticks_back, precision=highest)
    applied = kinetic[None, None] * psi_block + vpsi
    lowered = applied.astype(jnp.bfloat16)
    gathered = lax.all_gather(lowered, "band", axis=1, tiled=True)
    h_re = gathered[0].reshape(gathered.shape[1], -1)
    h_im = gathered[1].reshape(gathered.shape[1], -1)
    real_part = lax.dot_general(
        h_re, all_re, dims, preferred_element_type=jnp.float32
    ) + lax.dot_general(h_im, all_im, dims, preferred_element_type=jnp.float32)
    imag_part = lax.dot_general(
        h_re, all_im, dims, preferred_element_type=jnp.float32
    ) - lax.dot_general(h_im, all_re, dims, preferred_element_type=jnp.float32)
    partials = [jnp.stack([real_part, imag_part])]
    stacked = jnp.stack(partials, axis=1)
    stacked = stacked.reshape(2, group_count, band_count, 2, stacked.shape[-1])
    partial_value = jnp.transpose(stacked, (0, 2, 1, 3, 4)).reshape(
        2, band_count * local_bands, stacked.shape[-1]
    )
    summed = lax.psum(partial_value, "pw")
    cols_dev = partial_value.shape[1] // pw_count
    intersection = lax.dynamic_slice_in_dim(summed, rank * cols_dev, cols_dev, 1)
    return (intersection, applied)


def solution(mesh):
    return jax.shard_map(
        per_device,
        mesh=mesh,
        in_specs=(
            P(None, "band", "pw", None),
            P(None, "band", "pw", None),
            P("pw", None, None),
            P(),
        ),
        out_specs=(P(None, "pw", "band"), P(None, "band", "pw", None)),
        check_vma=False,
    )
```

profile of v0, /device:TPU:0, one launch (start us, length us, event | category | flops | bytes accessed | tf_op | source)
XLA Modules:
  0.0 115.9 jit_solution(15763958665738720233)
XLA Ops:
  2.2 1.2 %convolution_bitcast_fusion = f32[2,128,2,32]{1,3,0,2:T(8,128)S(1)} fusion(f32[1,2,128,128]{3,2,1,0:T(8,128)S(1)} %get-tuple-element.20, f32[1,2,128,128]{3,2,1,0:T(8,128)S(1)} %get-tuple-element.21, f32[2,2,32,128]{3,2,1,0:T(8,128)} %param.4), kind=kOutput, calls=%fused_computation.30 | convolution fusion | flops 50397184 | bytes 393216 | tf_op jit(solution)/shard_map/dcvu,cbsu->bvds/dot_general | solution.py:65
  3.6 0.9 reshape.230
  4.5 7.3 %all-to-all-start = ((f32[8,1,2048]{2,1,0:T(1,128)}), f32[8,1,2048]{2,1,0:T(1,128)}, u32[]{:S(2)}, u32[]{:S(2)}) async-start(f32[8,1,2048]{2,1,0:T(1,128)} %reshape.230), calls=%async_computation | async-start | bytes 131072 | tf_op jit(solution)/shard_map/all_to_all | solution.py:66
  11.8 1.2 %fusion.62 = (f32[128,256]{1,0:T(8,128)S(1)}, f32[128,256]{1,0:T(8,128)}) fusion(s32[256]{0:T(256)S(1)} %get-tuple-element.25), kind=kLoop, calls=%fused_computation.86 | loop fusion | flops 458752 | bytes 263168 | tf_op jit(solution)/shard_map/cos | solution.py:52
  13.0 1.1 multiply_bitcast_fusion
  14.1 4.3 %fusion.86 = (bf16[1,256,32,128]{3,2,1,0:T(8,128)(2,1)S(1)}, bf16[1,256,32,128]{3,2,1,0:T(8,128)(2,1)}) fusion(bf16[2,256,32,128]{3,2,1,0:T(8,128)(2,1)} %param.5), kind=kLoop, calls=%fused_computation.131 | loop fusion | bytes 8388608 | tf_op jit(solution)/shard_map/slice | solution.py:61
  18.4 1.6 %copy.66 = f32[16,128,128]{2,1,0:T(8,128)S(1)} copy(f32[16,128,128]{1,2,0:T(8,128)} %multiply_bitcast_fusion) | data formatting | bytes 2097152 | tf_op jit(solution)/shard_map/div | solution.py:56
  20.6 2.3 %reduce = f32[8,2048]{1,0:T(8,128)} reduce(f32[8,1,2048]{2,1,0:T(1,128)} %all-to-all-done, f32[]{:T(128)} %broadcast.384), dimensions={1}, to_apply=%all_to_all.26.reduce_sub_computation | reduce | bytes 131076 | tf_op jit(solution)/shard_map/all_to_all | solution.py:66
  22.8 1.8 %reshape.231 = f32[128,2,2,32]{3,2,1,0:T(2,128)} reshape(f32[8,2048]{1,0:T(8,128)} %reduce) | data formatting | bytes 131072
  24.6 1.0 copy.64
  25.6 0.8 copy.65
  26.4 1.7 %all_to_all.29 = f32[2,16,2,256]{3,1,2,0:T(8,128)} reshape(f32[2,16,2,8,32]{4,3,1,2,0:T(8,128)} %copy.65) | data formatting | bytes 131072 | tf_op jit(solution)/shard_map/all_to_all | solution.py:66
  28.1 0.8 slice_bitcast_fusion.11
  28.9 3.3 %fusion = f32[2,16,128,128]{3,2,1,0:T(8,128)S(1)} fusion(f32[128,256]{1,0:T(8,128)} %get-tuple-element.27, f32[2,16,256]{2,1,0:T(8,128)S(1)} %get-tuple-element.23, f32[128,256]{1,0:T(8,128)S(1)} %get-tuple-element.26, f32[2,16,256]{2,1,0:T(8,128)S(1)} %get-tuple-element.22, s32[256]{0:T(256)S(1)} %get-tuple-element.24), kind=kOutput, calls=%fused_computation.2 | convolution fusion | flops 1613791232 | bytes 2425856 | tf_op jit(solution)/shard_map/dot_general | solution.py:59
  32.3 2.5 %fusion.4 = f32[2,16,128,128]{3,2,1,0:T(8,128)S(1)} fusion(f32[128,256]{1,0:T(8,128)S(1)} %copy-done.1, f32[2,16,256]{2,1,0:T(8,128)S(1)} %get-tuple-element.23, f32[128,256]{1,0:T(8,128)S(1)} %get-tuple-element.26, f32[2,16,256]{2,1,0:T(8,128)S(1)} %get-tuple-element.22, s32[256]{0:T(256)S(1)} %get-tuple-element.24), kind=kOutput, calls=%fused_computation.6 | convolution fusion | flops 1613791232 | bytes 2425856 | tf_op jit(solution)/shard_map/dot_general | solution.py:59
  34.7 1.9 %fusion.72 = f32[2,16,128,128]{3,2,1,0:T(8,128)S(1)} fusion(f32[2,16,128,128]{3,2,1,0:T(8,128)S(1)} %fusion.4, f32[1,2,128,128]{3,2,1,0:T(8,128)S(1)} %get-tuple-element.20), kind=kOutput, calls=%fused_computation.96 | convolution fusion | flops 805306368 | bytes 4259840 | tf_op jit(solution)/shard_map/dot_general | solution.py:59
  36.6 1.8 %fusion.69 = f32[2,16,128,128]{3,2,1,0:T(8,128)S(1)} fusion(f32[2,16,128,128]{3,2,1,0:T(8,128)S(1)} %fusion.4, f32[1,2,128,128]{3,2,1,0:T(8,128)S(1)} %get-tuple-element.21), kind=kOutput, calls=%fused_computation.93 | convolution fusion | flops 805306368 | bytes 4259840 | tf_op jit(solution)/shard_map/dot_general | solution.py:59
  38.4 2.0 %subtract_multiply_fusion = f32[2,16,128,128]{3,2,1,0:T(8,128)S(1)} fusion(f32[2,16,128,128]{3,2,1,0:T(8,128)S(1)} %fusion.69, f32[2,16,128,128]{3,2,1,0:T(8,128)S(1)} %fusion, f32[16,128,128]{2,1,0:T(8,128)S(1)} %copy.66, f32[1,2,128,128]{3,2,1,0:T(8,128)S(1)} %get-tuple-element.20), kind=kOutput, calls=%fused_computation.17 | convolution fusion | flops 806354944 | bytes 7405568 | tf_op jit(solution)/shard_map/dot_general | solution.py:59
  40.4 1.8 %fusion.70 = f32[2,16,128,128]{3,2,1,0:T(8,128)S(1)} fusion(f32[2,16,128,128]{3,2,1,0:T(8,128)S(1)} %subtract_multiply_fusion, f32[1,2,128,128]{3,2,1,0:T(8,128)S(1)} %get-tuple-element.20), kind=kOutput, calls=%fused_computation.94 | convolution fusion | flops 805306368 | bytes 4259840 | tf_op jit(solution)/shard_map/dot_general | solution.py:59
  42.2 1.8 %fusion.68 = f32[2,16,128,128]{3,2,1,0:T(8,128)S(1)} fusion(f32[2,16,128,128]{3,2,1,0:T(8,128)S(1)} %subtract_multiply_fusion, f32[1,2,128,128]{3,2,1,0:T(8,128)S(1)} %get-tuple-element.21), kind=kOutput, calls=%fused_computation.92 | convolution fusion | flops 805306368 | bytes 4259840 | tf_op jit(solution)/shard_map/dot_general | solution.py:59
  44.0 1.9 %add_multiply_fusion = f32[2,16,128,128]{3,2,1,0:T(8,128)S(1)} fusion(f32[2,16,128,128]{3,2,1,0:T(8,128)S(1)} %fusion.72, f32[2,16,128,128]{3,2,1,0:T(8,128)S(1)} %fusion, f32[16,128,128]{2,1,0:T(8,128)S(1)} %copy.66, f32[1,2,128,128]{3,2,1,0:T(8,128)S(1)} %get-tuple-element.21), kind=kOutput, calls=%fused_computation.16 | convolution fusion | flops 806354944 | bytes 7405568 | tf_op jit(solution)/shard_map/dot_general | solution.py:59
  46.0 1.8 %fusion.67 = f32[2,16,128,128]{3,2,1,0:T(8,128)S(1)} fusion(f32[2,16,128,128]{3,2,1,0:T(8,128)S(1)} %add_multiply_fusion, f32[1,2,128,128]{3,2,1,0:T(8,128)S(1)} %get-tuple-element.21), kind=kOutput, calls=%fused_computation.91 | convolution fusion | flops 805306368 | bytes 4259840 | tf_op jit(solution)/shard_map/dot_general | solution.py:59
  47.7 1.8 %fusion.71 = f32[2,16,128,128]{3,2,1,0:T(8,128)S(1)} fusion(f32[2,16,128,128]{3,2,1,0:T(8,128)S(1)} %add_multiply_fusion, f32[1,2,128,128]{3,2,1,0:T(8,128)S(1)} %get-tuple-element.20), kind=kOutput, calls=%fused_computation.95 | convolution fusion | flops 805306368 | bytes 4259840 | tf_op jit(solution)/shard_map/dot_general | solution.py:59
  49.6 1.8 %fusion.10 = f32[2,16,128,256]{3,2,1,0:T(8,128)S(1)} fusion(f32[2,16,128,128]{3,2,1,0:T(8,128)S(1)} %fusion.68, f32[2,16,128,128]{3,2,1,0:T(8,128)S(1)} %fusion.71, s32[256]{0:T(256)S(1)} %get-tuple-element.24), kind=kOutput, calls=%fused_computation.14 | convolution fusion | flops 1611169792 | bytes 8389632 | tf_op jit(solution)/shard_map/dot_general | solution.py:59
  51.4 2.8 %add_reduce_fusion = (f32[2,16,256]{2,1,0:T(8,128)S(1)}, f32[2,16,256]{2,1,0:T(8,128)S(1)}) fusion(f32[2,16,128,256]{3,2,1,0:T(8,128)S(1)} %fusion.10, f32[128,256]{1,0:T(8,128)S(1)} %copy-done.1, f32[128,256]{1,0:T(8,128)S(1)} %get-tuple-element.26, s32[256]{0:T(256)S(1)} %get-tuple-element.24, f32[2,16,128,128]{3,2,1,0:T(8,128)S(1)} %fusion.67, ...), kind=kOutput, calls=%fused_computation.1 | convolution fusion | flops 1619542016 | bytes 8717312 | tf_op jit(solution)/shard_map/dot_general | solution.py:59
  54.5 1.4 %reshape.232 = f32[8,1,2048]{2,1,0:T(1,128)} reshape(f32[256,2,2,16]{3,2,1,0:T(2,128)S(1)} %bitcast.156) | data formatting | bytes 131072
  55.9 6.0 %all-to-all-start.1 = ((f32[8,1,2048]{2,1,0:T(1,128)}), f32[8,1,2048]{2,1,0:T(1,128)S(1)}, u32[]{:S(2)}, u32[]{:S(2)}) async-start(f32[8,1,2048]{2,1,0:T(1,128)} %reshape.232), calls=%async_computation.1 | async-start | bytes 131072 | tf_op jit(solution)/shard_map/all_to_all | solution.py:82
  62.0 6.8 %all-to-all-done.1 = f32[8,1,2048]{2,1,0:T(1,128)S(1)} async-done(((f32[8,1,2048]{2,1,0:T(1,128)}), f32[8,1,2048]{2,1,0:T(1,128)S(1)}, u32[]{:S(2)}, u32[]{:S(2)}) %all-to-all-start.1) | async-done | bytes 65568 | tf_op jit(solution)/shard_map/all_to_all | solution.py:82
  68.8 0.8 reduce.1
  71.9 5.4 %all_gather.3 = bf16[2,8,32,128]{3,2,0,1:T(8,128)(2,1)S(1)} all-gather(bf16[2,2,32,128]{3,2,0,1:T(8,128)(2,1)S(1)} %get-tuple-element.28), channel_id=1, replica_groups=mesh['pw'=8,'band'=4] {'band'}, dimensions={1}, use_global_device_ids=true | all-gather | bytes 163840 | tf_op jit(solution)/shard_map/all_gather | solution.py:86
  77.3 2.3 %fusion.26 = f32[8,256]{1,0:T(8,128)S(1)} fusion(bf16[1,256,32,128]{3,2,1,0:T(8,128)(2,1)} %get-tuple-element.15, bf16[1,8,32,128]{3,2,0,1:T(8,128)(2,1)S(1)} %get-tuple-element.17), kind=kOutput, calls=%fused_computation.34 | convolution fusion | flops 16777216 | bytes 2170880 | tf_op jit(solution)/shard_map/dot_general | solution.py:92
  81.7 33.7 %psum.7 = f32[2,8,256]{2,1,0:T(8,128)S(1)} all-reduce(f32[2,8,256]{2,1,0:T(8,128)S(1)} %pad_maximum_fusion.5), channel_id=1, replica_groups=mesh['pw'=8,'band'=4] {'pw'}, use_global_device_ids=true, to_apply=%region_2.3 | all-reduce | flops 4096 | bytes 32768 | tf_op jit(solution)/shard_map/psum | solution.py:101
  (37 shorter events, 7.7 us)
Async XLA Ops:
  0.6 11.2 %copy-start.6 = (s32[256]{0:T(256)S(1)}, s32[256]{0:T(256)}, u32[]{:S(2)}) copy-start(s32[256]{0:T(256)} %param.7) | copy-start | bytes 3076
  0.6 12.4 %copy-start.2 = (f32[16,128,128]{2,1,0:T(8,128)S(1)}, f32[16,128,128]{2,1,0:T(8,128)}, u32[]{:S(2)}) copy-start(f32[16,128,128]{2,1,0:T(8,128)} %param.6) | copy-start | bytes 3145732
  4.5 15.5 %all-to-all-start = ((f32[8,1,2048]{2,1,0:T(1,128)}), f32[8,1,2048]{2,1,0:T(1,128)}, u32[]{:S(2)}, u32[]{:S(2)}) async-start(f32[8,1,2048]{2,1,0:T(1,128)} %reshape.230), calls=%async_computation | async-start | bytes 131072 | tf_op jit(solution)/shard_map/all_to_all | solution.py:66
  28.1 4.2 %copy-start.1 = (f32[128,256]{1,0:T(8,128)S(1)}, f32[128,256]{1,0:T(8,128)}, u32[]{:S(2)}) copy-start(f32[128,256]{1,0:T(8,128)} %get-tuple-element.27) | copy-start | bytes 393220
  54.2 16.5 %copy-start.3 = (f32[1,2,128,128]{3,2,1,0:T(8,128)S(1)}, f32[1,2,128,128]{3,2,1,0:T(8,128)}, u32[]{:S(2)}) copy-start(f32[1,2,128,128]{3,2,1,0:T(8,128)} %get-tuple-element.18) | copy-start | bytes 393220
  54.2 16.5 %copy-start.4 = (f32[1,2,128,128]{3,2,1,0:T(8,128)S(1)}, f32[1,2,128,128]{3,2,1,0:T(8,128)}, u32[]{:S(2)}) copy-start(f32[1,2,128,128]{3,2,1,0:T(8,128)} %get-tuple-element.19) | copy-start | bytes 393220
  54.2 16.5 %copy-start.5 = (f32[2,2,32,128]{3,2,1,0:T(8,128)S(1)}, f32[2,2,32,128]{3,2,1,0:T(8,128)}, u32[]{:S(2)}) copy-start(f32[2,2,32,128]{3,2,1,0:T(8,128)} %param.4) | copy-start | bytes 196612
  55.9 12.9 %all-to-all-start.1 = ((f32[8,1,2048]{2,1,0:T(1,128)}), f32[8,1,2048]{2,1,0:T(1,128)S(1)}, u32[]{:S(2)}, u32[]{:S(2)}) async-start(f32[8,1,2048]{2,1,0:T(1,128)} %reshape.232), calls=%async_computation.1 | async-start | bytes 131072 | tf_op jit(solution)/shard_map/all_to_all | solution.py:82
  70.6 9.0 %copy-start = (bf16[1,256,32,128]{3,2,1,0:T(8,128)(2,1)S(1)}, bf16[1,256,32,128]{3,2,1,0:T(8,128)(2,1)}, u32[]{:S(2)}) copy-start(bf16[1,256,32,128]{3,2,1,0:T(8,128)(2,1)} %get-tuple-element.15) | copy-start | bytes 6291460
where the time goes:
time: 117 us; the launch traced here: 116 us
  blocking collectives  39.1 us (33%)
  matrix products  31.3 us (27%)
  local copies, waits for them, and re-layouts  17.5 us (15%)
  starting transfers between devices  13.3 us (11%)
  other arithmetic  7.07 us (6%)
  waiting for transfers between devices  6.84 us (6%)
    psum x1, blocking collectives, per_device(): summed = lax.psum(partial_value, 'pw')  33.7 us
    dot_general x12, matrix products, mult(): jnp.dot(left, right, precision=highest, preferred_element_type=jnp.float32)  25.2 us
    all_to_all x1, starting transfers between devices, per_device(): lax.all_to_all(z_lines, 'pw', split_axis=1, concat_axis=3, tiled=True)  7.28 us
    all_to_all x1, waiting for transfers between devices, per_device(): lax.all_to_all(picked, 'pw', split_axis=3, concat_axis=1, tiled=True)  6.83 us
    all_to_all x1, starting transfers between devices, per_device(): lax.all_to_all(picked, 'pw', split_axis=3, concat_axis=1, tiled=True)  5.99 us
    unnamed x19, local copies, waits for them, and re-layouts  5.42 us
    all_gather x1, blocking collectives, per_device(): gathered = lax.all_gather(lowered, 'band', axis=1, tiled=True)  5.41 us
    slice x1, local copies, waits for them, and re-layouts, per_device(): all_re = psi_all[0].reshape(psi_all.shape[1], -1)  4.29 us
  transfers between devices with their start and end apart: 2, of which 1 were waited for; matrix products, arithmetic and copies ran while one was open for 7% of the time, Pallas kernels for 0%

commit v1 on v0

--- a/solution.py
+++ b/solution.py
@@ -27,6 +27,22 @@
 
 
 def per_device(psi_block, psi_all, potential, stick_col):
+
+    def load_types(own_rows, chip_axis):
+        axis_len = lax.axis_size(chip_axis)
+        sides = list(map(lambda d: (d, (d + 1) % axis_len), range(axis_len)))
+        pieces_in = list(map(lambda d: (d, (d - 1) % axis_len), range(axis_len)))
+        tall, local_part = ([own_rows], [own_rows])
+        for _ in range(axis_len // 2):
+            tall.append(lax.ppermute(tall[-1], axis_name=chip_axis, perm=sides))
+        for _ in tuple(range((axis_len - 1) // 2)):
+            local_part.append(lax.ppermute(local_part[-1], axis_name=chip_axis, perm=pieces_in))
+        p_next = jnp.concatenate([*tall[::-1], *local_part[1:]], axis=1)
+        carry_in = jnp.roll(
+            p_next, shift=(lax.axis_index(chip_axis) - axis_len // 2) * own_rows.shape[1], axis=1
+        )
+        return carry_in
+
     local_bands = psi_block.shape[1]
     sticks_dev = psi_block.shape[2]
     grid_size = psi_block.shape[3]
@@ -83,7 +99,7 @@
     vpsi = jnp.einsum("dcvu,bucs->dbsv", forward, sticks_back, precision=highest)
     applied = kinetic[None, None] * psi_block + vpsi
     lowered = applied.astype(jnp.bfloat16)
-    gathered = lax.all_gather(lowered, "band", axis=1, tiled=True)
+    gathered = load_types(lowered, "band")
     h_re = gathered[0].reshape(gathered.shape[1], -1)
     h_im = gathered[1].reshape(gathered.shape[1], -1)
     real_part = lax.dot_general(

time: 117 us -> 107 us (0.915)
  waiting for transfers between devices: 6.84 us -> 16.8 us
  local copies, waits for them, and re-layouts: 17.5 us -> 10.7 us
  blocking collectives: 39.1 us -> 33.7 us
  other arithmetic: 7.07 us -> 3.25 us
  matrix products: 31.3 us -> 28.9 us
    all_to_all x1, waiting for transfers between devices: 0.01 us -> 5.79 us  [per_device(): lax.all_to_all(z_lines, 'pw', split_axis=1, concat_axis=3, tiled=True)]
    all_gather x1 -> x0, blocking collectives: 5.41 us -> none  [per_device(): gathered = lax.all_gather(lowered, 'band', axis=1, tiled=True)]
    ppermute x0 -> x3, waiting for transfers between devices: none -> 4.26 us  [the longest x2 3.33 us: load_types(): tall.append(lax.ppermute(tall[-1], axis_name=chip_axis, perm=sides))]
    all_to_all x4, local copies, waits for them, and re-layouts: 3.97 us -> 0.74 us  [per_device(): lax.all_to_all(z_lines, 'pw', split_axis=1, concat_axis=3, tiled=True)]
    all_to_all x1, starting transfers between devices: 5.99 us -> 3.35 us  [per_device(): lax.all_to_all(picked, 'pw', split_axis=3, concat_axis=1, tiled=True)]
    ppermute x0 -> x3, starting transfers between devices: none -> 1.8 us  [the longest x1 1.74 us: load_types(): lax.ppermute(local_part[-1], axis_name=chip_axis, perm=pieces_in)]
    dot_general x1, matrix products: 2.28 us -> 0.7 us  [per_device(): lax.dot_general(h_re, all_im, dims, preferred_element_type=jnp.float32)]
    unnamed x19 -> x20, local copies, waits for them, and re-layouts: 5.42 us -> 3.93 us
  transfers between devices with their start and end apart: 2 -> 5, of which waited for: 1 -> 4; matrix products, arithmetic and copies ran while one was open for 7% -> 6% of each run, Pallas kernels for 0% -> 0%
where the time goes in v1:
time: 107 us
  blocking collectives  33.7 us (31%)
  matrix products  28.9 us (27%)
  waiting for transfers between devices  16.8 us (16%)
  starting transfers between devices  12.4 us (12%)
  local copies, waits for them, and re-layouts  10.7 us (10%)
  other arithmetic  3.25 us (3%)
    psum x1, blocking collectives, per_device(): summed = lax.psum(partial_value, 'pw')  33.7 us
    dot_general x12, matrix products, mult(): jnp.dot(left, right, precision=highest, preferred_element_type=jnp.float32)  24.4 us
    all_to_all x1, starting transfers between devices, per_device(): lax.all_to_all(z_lines, 'pw', split_axis=1, concat_axis=3, tiled=True)  7.28 us
    all_to_all x1, waiting for transfers between devices, per_device(): lax.all_to_all(picked, 'pw', split_axis=3, concat_axis=1, tiled=True)  6.77 us
    all_to_all x1, waiting for transfers between devices, per_device(): lax.all_to_all(z_lines, 'pw', split_axis=1, concat_axis=3, tiled=True)  5.79 us
    slice x1, local copies, waits for them, and re-layouts, per_device(): all_im = psi_all[1].reshape(psi_all.shape[1], -1)  4.3 us
    unnamed x20, local copies, waits for them, and re-layouts  3.93 us
    all_to_all x1, starting transfers between devices, per_device(): lax.all_to_all(picked, 'pw', split_axis=3, concat_axis=1, tiled=True)  3.35 us
  transfers between devices with their start and end apart: 5, of which 4 were waited for; matrix products, arithmetic and copies ran while one was open for 6% of the time, Pallas kernels for 0%

profile of v1, /device:TPU:0, one launch (start us, length us, event | category | flops | bytes accessed | tf_op | source)
XLA Modules:
  0.0 106.8 jit_solution(7088719237774027668)
XLA Ops:
  1.5 1.2 %convolution_bitcast_fusion = f32[2,128,2,32]{1,3,0,2:T(8,128)S(1)} fusion(f32[1,2,128,128]{3,2,1,0:T(8,128)S(1)} %get-tuple-element.20, f32[1,2,128,128]{3,2,1,0:T(8,128)S(1)} %get-tuple-element.21, f32[2,2,32,128]{3,2,1,0:T(8,128)} %param.4), kind=kOutput, calls=%fused_computation.30 | convolution fusion | flops 50397184 | bytes 393216 | tf_op jit(solution)/shard_map/dcvu,cbsu->bvds/dot_general | solution.py:81
  2.9 0.9 reshape.230
  3.8 7.3 %all-to-all-start = ((f32[8,1,2048]{2,1,0:T(1,128)}), f32[8,1,2048]{2,1,0:T(1,128)S(1)}, u32[]{:S(2)}, u32[]{:S(2)}) async-start(f32[8,1,2048]{2,1,0:T(1,128)} %reshape.230), calls=%async_computation | async-start | bytes 131072 | tf_op jit(solution)/shard_map/all_to_all | solution.py:82
  12.2 5.8 %all-to-all-done = f32[8,1,2048]{2,1,0:T(1,128)S(1)} async-done(((f32[8,1,2048]{2,1,0:T(1,128)}), f32[8,1,2048]{2,1,0:T(1,128)S(1)}, u32[]{:S(2)}, u32[]{:S(2)}) %all-to-all-start) | async-done | bytes 65568 | tf_op jit(solution)/shard_map/all_to_all | solution.py:82
  18.5 0.8 reduce
  19.8 2.4 %fusion = f32[2,16,128,128]{3,2,1,0:T(8,128)S(1)} fusion(f32[128,256]{1,0:T(8,128)S(1)} %get-tuple-element.27, f32[2,16,256]{2,1,0:T(8,128)S(1)} %get-tuple-element.23, f32[128,256]{1,0:T(8,128)S(1)} %get-tuple-element.26, f32[2,16,256]{2,1,0:T(8,128)S(1)} %get-tuple-element.22, s32[256]{0:T(256)S(1)} %get-tuple-element.24), kind=kOutput, calls=%fused_computation.2 | convolution fusion | flops 1613791232 | bytes 2425856 | tf_op jit(solution)/shard_map/dot_general | solution.py:75
  22.3 2.4 %fusion.4 = f32[2,16,128,128]{3,2,1,0:T(8,128)S(1)} fusion(f32[128,256]{1,0:T(8,128)S(1)} %get-tuple-element.27, f32[2,16,256]{2,1,0:T(8,128)S(1)} %get-tuple-element.23, f32[128,256]{1,0:T(8,128)S(1)} %get-tuple-element.26, f32[2,16,256]{2,1,0:T(8,128)S(1)} %get-tuple-element.22, s32[256]{0:T(256)S(1)} %get-tuple-element.24), kind=kOutput, calls=%fused_computation.6 | convolution fusion | flops 1613791232 | bytes 2425856 | tf_op jit(solution)/shard_map/dot_general | solution.py:75
  24.7 1.8 %fusion.76 = f32[2,16,128,128]{3,2,1,0:T(8,128)S(1)} fusion(f32[2,16,128,128]{3,2,1,0:T(8,128)S(1)} %fusion.4, f32[1,2,128,128]{3,2,1,0:T(8,128)S(1)} %get-tuple-element.20), kind=kOutput, calls=%fused_computation.100 | convolution fusion | flops 805306368 | bytes 4259840 | tf_op jit(solution)/shard_map/dot_general | solution.py:75
  26.6 1.8 %fusion.73 = f32[2,16,128,128]{3,2,1,0:T(8,128)S(1)} fusion(f32[2,16,128,128]{3,2,1,0:T(8,128)S(1)} %fusion.4, f32[1,2,128,128]{3,2,1,0:T(8,128)S(1)} %get-tuple-element.21), kind=kOutput, calls=%fused_computation.97 | convolution fusion | flops 805306368 | bytes 4259840 | tf_op jit(solution)/shard_map/dot_general | solution.py:75
  28.4 1.9 %subtract_multiply_fusion = f32[2,16,128,128]{3,2,1,0:T(8,128)S(1)} fusion(f32[2,16,128,128]{3,2,1,0:T(8,128)S(1)} %fusion.73, f32[2,16,128,128]{3,2,1,0:T(8,128)S(1)} %fusion, f32[16,128,128]{2,1,0:T(8,128)S(1)} %copy.70, f32[1,2,128,128]{3,2,1,0:T(8,128)S(1)} %get-tuple-element.20), kind=kOutput, calls=%fused_computation.17 | convolution fusion | flops 806354944 | bytes 7405568 | tf_op jit(solution)/shard_map/dot_general | solution.py:75
  30.4 2.0 %fusion.74 = f32[2,16,128,128]{3,2,1,0:T(8,128)S(1)} fusion(f32[2,16,128,128]{3,2,1,0:T(8,128)S(1)} %subtract_multiply_fusion, f32[1,2,128,128]{3,2,1,0:T(8,128)S(1)} %get-tuple-element.20), kind=kOutput, calls=%fused_computation.98 | convolution fusion | flops 805306368 | bytes 4259840 | tf_op jit(solution)/shard_map/dot_general | solution.py:75
  32.4 1.8 %fusion.72 = f32[2,16,128,128]{3,2,1,0:T(8,128)S(1)} fusion(f32[2,16,128,128]{3,2,1,0:T(8,128)S(1)} %subtract_multiply_fusion, f32[1,2,128,128]{3,2,1,0:T(8,128)S(1)} %get-tuple-element.21), kind=kOutput, calls=%fused_computation.96 | convolution fusion | flops 805306368 | bytes 4259840 | tf_op jit(solution)/shard_map/dot_general | solution.py:75
  34.2 1.9 %add_multiply_fusion = f32[2,16,128,128]{3,2,1,0:T(8,128)S(1)} fusion(f32[2,16,128,128]{3,2,1,0:T(8,128)S(1)} %fusion.76, f32[2,16,128,128]{3,2,1,0:T(8,128)S(1)} %fusion, f32[16,128,128]{2,1,0:T(8,128)S(1)} %copy.70, f32[1,2,128,128]{3,2,1,0:T(8,128)S(1)} %get-tuple-element.21), kind=kOutput, calls=%fused_computation.16 | convolution fusion | flops 806354944 | bytes 7405568 | tf_op jit(solution)/shard_map/dot_general | solution.py:75
  36.1 1.8 %fusion.71 = f32[2,16,128,128]{3,2,1,0:T(8,128)S(1)} fusion(f32[2,16,128,128]{3,2,1,0:T(8,128)S(1)} %add_multiply_fusion, f32[1,2,128,128]{3,2,1,0:T(8,128)S(1)} %get-tuple-element.21), kind=kOutput, calls=%fused_computation.95 | convolution fusion | flops 805306368 | bytes 4259840 | tf_op jit(solution)/shard_map/dot_general | solution.py:75
  37.9 1.8 %fusion.75 = f32[2,16,128,128]{3,2,1,0:T(8,128)S(1)} fusion(f32[2,16,128,128]{3,2,1,0:T(8,128)S(1)} %add_multiply_fusion, f32[1,2,128,128]{3,2,1,0:T(8,128)S(1)} %get-tuple-element.20), kind=kOutput, calls=%fused_computation.99 | convolution fusion | flops 805306368 | bytes 4259840 | tf_op jit(solution)/shard_map/dot_general | solution.py:75
  39.8 1.8 %fusion.10 = f32[2,16,128,256]{3,2,1,0:T(8,128)S(1)} fusion(f32[2,16,128,128]{3,2,1,0:T(8,128)S(1)} %fusion.72, f32[2,16,128,128]{3,2,1,0:T(8,128)S(1)} %fusion.75, s32[256]{0:T(256)S(1)} %get-tuple-element.24), kind=kOutput, calls=%fused_computation.14 | convolution fusion | flops 1611169792 | bytes 8389632 | tf_op jit(solution)/shard_map/dot_general | solution.py:75
  41.6 2.8 %add_reduce_fusion = (f32[2,16,256]{2,1,0:T(8,128)S(1)}, f32[2,16,256]{2,1,0:T(8,128)S(1)}) fusion(f32[2,16,128,256]{3,2,1,0:T(8,128)S(1)} %fusion.10, f32[128,256]{1,0:T(8,128)S(1)} %get-tuple-element.27, f32[128,256]{1,0:T(8,128)S(1)} %get-tuple-element.26, s32[256]{0:T(256)S(1)} %get-tuple-element.24, f32[2,16,128,128]{3,2,1,0:T(8,128)S(1)} %fusion.71, ...), kind=kOutput, calls=%fused_computation.1 | convolution fusion | flops 1619542016 | bytes 8717312 | tf_op jit(solution)/shard_map/dot_general | solution.py:75
  44.7 1.4 %reshape.232 = f32[8,1,2048]{2,1,0:T(1,128)} reshape(f32[256,2,2,16]{3,2,1,0:T(2,128)S(1)} %bitcast.152) | data formatting | bytes 131072
  46.1 3.4 %all-to-all-start.1 = ((f32[8,1,2048]{2,1,0:T(1,128)}), f32[8,1,2048]{2,1,0:T(1,128)S(1)}, u32[]{:S(2)}, u32[]{:S(2)}) async-start(f32[8,1,2048]{2,1,0:T(1,128)} %reshape.232), calls=%async_computation.1 | async-start | bytes 131072 | tf_op jit(solution)/shard_map/all_to_all | solution.py:98
  49.5 6.8 %all-to-all-done.1 = f32[8,1,2048]{2,1,0:T(1,128)S(1)} async-done(((f32[8,1,2048]{2,1,0:T(1,128)}), f32[8,1,2048]{2,1,0:T(1,128)S(1)}, u32[]{:S(2)}, u32[]{:S(2)}) %all-to-all-start.1) | async-done | bytes 65568 | tf_op jit(solution)/shard_map/all_to_all | solution.py:98
  56.3 0.8 reduce.1
  57.1 0.7 reshape.233
  58.8 3.3 %collective-permute-done = bf16[2,2,32,128]{3,2,0,1:T(8,128)(2,1)S(1)} collective-permute-done((bf16[2,2,32,128]{3,2,0,1:T(8,128)(2,1)S(1)}, bf16[2,2,32,128]{3,2,0,1:T(8,128)(2,1)S(1)}, u32[]{:S(2)}, u32[]{:S(2)}) %collective-permute-start) | collective-permute-done | bytes 32800 | tf_op jit(solution)/shard_map/ppermute | solution.py:37
  62.1 4.3 %fusion.90 = (bf16[1,256,32,128]{3,2,1,0:T(8,128)(2,1)S(1)}, bf16[1,256,32,128]{3,2,1,0:T(8,128)(2,1)}) fusion(bf16[2,256,32,128]{3,2,1,0:T(8,128)(2,1)} %param.5), kind=kLoop, calls=%fused_computation.143 | loop fusion | bytes 8388608 | tf_op jit(solution)/shard_map/slice | solution.py:78
  66.4 1.7 %collective-permute-start.2 = (bf16[2,2,32,128]{3,2,0,1:T(8,128)(2,1)S(1)}, bf16[2,2,32,128]{3,2,0,1:T(8,128)(2,1)S(1)}, u32[]{:S(2)}, u32[]{:S(2)}) collective-permute-start(bf16[2,2,32,128]{3,2,0,1:T(8,128)(2,1)S(1)} %get-tuple-element.28), channel_id=1, source_target_pairs={{0,3},{1,0},{2,1},{3,2},{4,7},{5,4},{6,5},{7,6},{8,11},{9,8},{10,9... | collective-permute-start | bytes 98312 | tf_op jit(solution)/shard_map/ppermute | solution.py:39
  68.1 0.6 copy.81
  68.8 0.9 collective-permute-done.2
  69.8 0.7 fusion.25
  70.5 0.7 fusion.28
  71.2 0.7 fusion.30
  71.9 0.7 fusion.32
  72.6 33.7 %psum.7 = f32[2,8,256]{2,1,0:T(8,128)S(1)} all-reduce(f32[2,8,256]{2,1,0:T(8,128)S(1)} %pad_maximum_fusion.5), channel_id=1, replica_groups=mesh['pw'=8,'band'=4] {'pw'}, use_global_device_ids=true, to_apply=%region_2.3 | all-reduce | flops 4096 | bytes 32768 | tf_op jit(solution)/shard_map/psum | solution.py:117
  (44 shorter events, 5.1 us)
Async XLA Ops:
  0.6 10.5 %copy-start.3 = (s32[256]{0:T(256)S(1)}, s32[256]{0:T(256)}, u32[]{:S(2)}) copy-start(s32[256]{0:T(256)} %param.7) | copy-start | bytes 3076
  0.6 11.0 %copy-start.1 = (f32[16,128,128]{2,1,0:T(8,128)S(1)}, f32[16,128,128]{2,1,0:T(8,128)}, u32[]{:S(2)}) copy-start(f32[16,128,128]{2,1,0:T(8,128)} %param.6) | copy-start | bytes 3145732
  3.8 14.2 %all-to-all-start = ((f32[8,1,2048]{2,1,0:T(1,128)}), f32[8,1,2048]{2,1,0:T(1,128)S(1)}, u32[]{:S(2)}, u32[]{:S(2)}) async-start(f32[8,1,2048]{2,1,0:T(1,128)} %reshape.230), calls=%async_computation | async-start | bytes 131072 | tf_op jit(solution)/shard_map/all_to_all | solution.py:82
  44.4 13.7 %copy-start.2 = (f32[2,2,32,128]{3,2,1,0:T(8,128)S(1)}, f32[2,2,32,128]{3,2,1,0:T(8,128)}, u32[]{:S(2)}) copy-start(f32[2,2,32,128]{3,2,1,0:T(8,128)} %param.4) | copy-start | bytes 196612
  46.1 10.2 %all-to-all-start.1 = ((f32[8,1,2048]{2,1,0:T(1,128)}), f32[8,1,2048]{2,1,0:T(1,128)S(1)}, u32[]{:S(2)}, u32[]{:S(2)}) async-start(f32[8,1,2048]{2,1,0:T(1,128)} %reshape.232), calls=%async_computation.1 | async-start | bytes 131072 | tf_op jit(solution)/shard_map/all_to_all | solution.py:98
  58.7 3.4 %collective-permute-start = (bf16[2,2,32,128]{3,2,0,1:T(8,128)(2,1)S(1)}, bf16[2,2,32,128]{3,2,0,1:T(8,128)(2,1)S(1)}, u32[]{:S(2)}, u32[]{:S(2)}) collective-permute-start(bf16[2,2,32,128]{3,2,0,1:T(8,128)(2,1)S(1)} %get-tuple-element.28), channel_id=1, source_target_pairs={{0,1},{1,2},{2,3},{3,0},{4,5},{5,6},{6,7},{7,4},{8,9},{9,10},{10,1... | collective-permute-start | bytes 98312 | tf_op jit(solution)/shard_map/ppermute | solution.py:37
  62.1 6.7 %collective-permute-start.1 = (bf16[2,2,32,128]{3,2,0,1:T(8,128)(2,1)S(1)}, bf16[2,2,32,128]{3,2,0,1:T(8,128)(2,1)S(1)}, u32[]{:S(2)}, u32[]{:S(2)}) collective-permute-start(bf16[2,2,32,128]{3,2,0,1:T(8,128)(2,1)S(1)} %collective-permute-done), channel_id=1, source_target_pairs={{0,1},{1,2},{2,3},{3,0},{4,5},{5,6},{6,7},{7,4},{8,9},{9,10},{10,1... | collective-permute-start | bytes 98312 | tf_op jit(solution)/shard_map/ppermute | solution.py:37
  66.4 4.1 %copy-start = (bf16[1,256,32,128]{3,2,1,0:T(8,128)(2,1)S(1)}, bf16[1,256,32,128]{3,2,1,0:T(8,128)(2,1)}, u32[]{:S(2)}) copy-start(bf16[1,256,32,128]{3,2,1,0:T(8,128)(2,1)} %get-tuple-element.15) | copy-start | bytes 6291460
  66.4 3.3 %collective-permute-start.2 = (bf16[2,2,32,128]{3,2,0,1:T(8,128)(2,1)S(1)}, bf16[2,2,32,128]{3,2,0,1:T(8,128)(2,1)S(1)}, u32[]{:S(2)}, u32[]{:S(2)}) collective-permute-start(bf16[2,2,32,128]{3,2,0,1:T(8,128)(2,1)S(1)} %get-tuple-element.28), channel_id=1, source_target_pairs={{0,3},{1,0},{2,1},{3,2},{4,7},{5,4},{6,5},{7,6},{8,11},{9,8},{10,9... | collective-permute-start | bytes 98312 | tf_op jit(solution)/shard_map/ppermute | solution.py:39
